TPU v7x, 32 devices: a whole 2x2x4 slice. The times are simulated.
32 devices in a mesh: section: 2 (over x), mp: 4 (over z), dp: 4 (over y, core).
Axes of the slice: x: 2, y: 2, z: 4, core: 2. Of those that a mesh axis runs over, the one named last changes fastest.
Arguments:
- text_in: bfloat16 [4, 2, 512, 8192], P('dp', 'section', None, 'mp'), may hold values from -6 to 6
- vision: bfloat16 [4, 2, 256, 8192], P('dp', 'section', None, 'mp'), may hold values from -6 to 6
- tile_counts: int32 [4, 2], P('dp'), may hold values from 1 to 4, as said below
- lengths: int32 [4, 2], P('dp', 'section'), may hold values from 128 to 512, as said below
- image_of: int32 [4, 2], P('dp'), may hold values from 0 to 1, each once within a row
- norm_gain: float32 [2, 8192], P('section'), may hold values from 0.5 to 1.5
- query_weight: bfloat16 [2, 8192, 4096], P('section', 'dp', 'mp'), may hold values from -0.0625 to 0.0625
- key_weight: bfloat16 [2, 8192, 1024], P('section', 'dp', 'mp'), may hold values from -0.0625 to 0.0625
- value_weight: bfloat16 [2, 8192, 1024], P('section', 'dp', 'mp'), may hold values from -0.0625 to 0.0625
- query_gain: float32 [2, 128], P('section')
- key_gain: float32 [2, 128], P('section')
- cross_gate: float32 [2], P('section'), may hold values from 0.4 to 1.5
- context_grad: bfloat16 [4, 2, 512, 4096], P('dp', 'section', None, 'mp'), may hold values from -6 to 6
Outputs:
- gated_context: bfloat16 [4, 2, 512, 4096], P('dp', 'section', None, 'mp')
- vision_grad: bfloat16 [4, 2, 256, 8192], P('dp', 'section', None, 'mp')
- key_weight_grad: bfloat16 [2, 8192, 1024], P('section', 'dp', 'mp')
- value_weight_grad: bfloat16 [2, 8192, 1024], P('section', 'dp', 'mp')
Inputs may be any that keep to these rules, and one draw needn't show every extreme that they name: `tile_counts`: some image has 4 tiles and some has one. `lengths`: some sample has the full 512 tokens. `image_of`: each row is a permutation of the sections.
All inputs are finite; a program needn't handle non-finite values.
Results may differ from a plain program's by a relative error of at most 0.018.
Values may be sent and summed in bfloat16 or wider, within the bound.
No kernel may reach another device: no remote copies, remote signals or barrier semaphores. Data moves between devices by JAX's collectives and lax.ppermute only.
A program may use at most 192 MiB of HBM per device.

v0:
```python
import jax
import jax.numpy as jnp
from jax import lax
from jax.sharding import PartitionSpec as P

HD = 128
TILE_ROWS = 64


def shifted(value, axis, steps):
    count = lax.axis_size(axis)
    pairs = [(source, (source + steps) % count) for source in range(count)]
    return lax.ppermute(value, axis, pairs)


def norm_rows(values, gain):
    values = values.astype(jnp.float32)
    scaled = values * lax.rsqrt(jnp.mean(values * values, axis=-1, keepdims=True) + 1e-05)
    return scaled * gain


def rounded(values):
    return lax.optimization_barrier(values.astype(jnp.bfloat16)).astype(jnp.float32)


def attend(queries, keys_raw, values_raw, key_norm, usable, present, gate_value):
    keys = rounded(norm_rows(keys_raw, key_norm))
    values = rounded(values_raw)
    text_rows, heads, depth = queries.shape
    groups = keys.shape[1]
    grouped = queries.astype(jnp.float32).reshape(text_rows, groups, heads // groups, depth)
    scores = jnp.einsum("tgjd,vgd->gjtv", grouped, keys) * depth ** (-0.5)
    scores = jnp.where(usable[None, None, None, :], scores, -1e30)
    highest = lax.stop_gradient(jnp.max(scores, axis=-1, keepdims=True))
    weights = jnp.exp(scores - highest)
    probs = rounded(weights / jnp.sum(weights, axis=-1, keepdims=True))
    context = jnp.einsum("gjtv,vgd->tgjd", probs, values).reshape(text_rows, heads * depth)
    return jnp.where(present[:, None], jnp.tanh(gate_value) * context, 0.0)


def per_device(
    text_in,
    vision,
    tile_counts,
    lengths,
    image_of,
    norm_gain,
    query_weight,
    key_weight,
    value_weight,
    query_gain,
    key_gain,
    cross_gate,
    context_grad,
):
    arrived = shifted(text_in, "section", 1)
    full_text = lax.all_gather(arrived, "mp", axis=3, tiled=True)[0, 0]
    text_rows = full_text.shape[0]
    normed = norm_rows(full_text, norm_gain[0]).astype(jnp.bfloat16)
    width_q = query_weight.shape[2]
    columns = normed
    query_raw = jnp.dot(
        columns,
        lax.all_gather(query_weight, "dp", axis=1, tiled=True)[0],
        preferred_element_type=jnp.float32,
    )
    queries = norm_rows(query_raw.reshape(text_rows, width_q // HD, HD), query_gain[0]).astype(
        jnp.bfloat16
    )
    key_full, value_full = (
        lax.all_gather(key_weight, "dp", axis=1, tiled=True),
        lax.all_gather(value_weight, "dp", axis=1, tiled=True),
    )
    key_full = key_full[0]
    value_full = value_full[0]
    slot_rows = vision.shape[2]
    part_width = vision.shape[3]
    wanted = image_of[0, lax.axis_index("section")]
    shard_piece = lax.all_gather(vision, "section", axis=1, tiled=True)
    owners = jnp.arange(shard_piece.shape[1])
    chosen = (owners == wanted)[:, None, None]
    taken = jnp.where(chosen, shard_piece[0], jnp.zeros_like(shard_piece[0]))
    image_part = jnp.sum(taken.astype(jnp.float32), axis=0).astype(jnp.bfloat16)
    image = lax.all_gather(image_part, "mp", axis=1, tiled=True)
    width_k = key_full.shape[1]
    keys_raw = jnp.dot(image, key_full, preferred_element_type=jnp.float32).reshape(
        slot_rows, width_k // HD, HD
    )
    values_raw = jnp.dot(image, value_full, preferred_element_type=jnp.float32).reshape(
        slot_rows, width_k // HD, HD
    )
    usable = jnp.arange(slot_rows) < tile_counts[0, wanted] * TILE_ROWS
    present = jnp.arange(text_rows) < lengths[0, 0]

    def forward(keys_in, values_in):
        return attend(queries, keys_in, values_in, key_gain[0], usable, present, cross_gate[0])

    context, pullback = jax.vjp(forward, keys_raw, values_raw)
    gated_context = context.astype(jnp.bfloat16).reshape(1, 1, text_rows, width_q)
    key_back, value_back = pullback(context_grad[0, 0].astype(jnp.float32))
    key_flat = key_back.reshape(slot_rows, width_k).astype(jnp.bfloat16)
    value_flat = value_back.reshape(slot_rows, width_k).astype(jnp.bfloat16)
    contract = (((1,), (1,)), ((), ()))
    partial_sum = lax.dot_general(key_flat, key_full, contract, preferred_element_type=jnp.float32)
    partial_sum = partial_sum + lax.dot_general(
        value_flat, value_full, contract, preferred_element_type=jnp.float32
    )
    partial_bf = partial_sum.astype(jnp.bfloat16)
    summed = lax.psum_scatter(
        partial_bf.astype(jnp.float32).astype(jnp.bfloat16), "mp", scatter_dimension=1, tiled=True
    )
    row_ids = jnp.arange(slot_rows * lax.axis_size("section"))
    taken = jnp.take(summed, row_ids % slot_rows, axis=0).astype(jnp.float32)
    routed = lax.psum_scatter(
        jnp.where((row_ids // slot_rows == wanted)[:, None], taken, 0.0).astype(jnp.bfloat16),
        "section",
        scatter_dimension=0,
        tiled=True,
    )
    vision_grad = routed.reshape(1, 1, slot_rows, part_width)
    columns = image
    inner = (((0,), (0,)), ((), ()))
    key_part = lax.dot_general(columns, key_flat, inner, preferred_element_type=jnp.float32).astype(
        jnp.bfloat16
    )
    value_part = lax.dot_general(
        columns, value_flat, inner, preferred_element_type=jnp.float32
    ).astype(jnp.bfloat16)
    both_grads = lax.psum_scatter(
        jnp.concatenate([key_part, value_part], axis=1).astype(jnp.float32).astype(jnp.bfloat16),
        "dp",
        scatter_dimension=0,
        tiled=True,
    )
    key_weight_grad = both_grads[:, :width_k][None]
    value_weight_grad = both_grads[:, width_k:][None]
    return (gated_context, vision_grad, key_weight_grad, value_weight_grad)


def solution(mesh):
    return jax.shard_map(
        per_device,
        mesh=mesh,
        in_specs=(
            P("dp", "section", None, "mp"),
            P("dp", "section", None, "mp"),
            P("dp", None),
            P("dp", "section"),
            P("dp", None),
            P("section", None),
            P("section", "dp", "mp"),
            P("section", "dp", "mp"),
            P("section", "dp", "mp"),
            P("section", None),
            P("section", None),
            P("section"),
            P("dp", "section", None, "mp"),
        ),
        out_specs=(
            P("dp", "section", None, "mp"),
            P("dp", "section", None, "mp"),
            P("section", "dp", "mp"),
            P("section", "dp", "mp"),
        ),
        check_vma=False,
    )
```

profile of v0, /device:TPU:0, one launch (start us, length us, event | category | flops | bytes accessed | tf_op | source)
XLA Modules:
  0.0 705.0 jit_solution(10474390815657424555)
XLA Ops:
  10.7 34.7 %all-gather.7.cloned.1.call-done = bf16[1,2,256,2048]{3,2,0,1:T(8,128)(2,1)} async-done(((bf16[1,1,256,2048]{3,2,0,1:T(8,128)(2,1)}), bf16[1,2,256,2048]{3,2,0,1:T(8,128)(2,1)}) %all-gather.7.cloned.1.call-update) | async-done | bytes 2097168 | tf_op jit(solution)/shard_map/all_gather | solution.py:79
  45.4 3.4 fusion.34
  49.3 47.3 %collective-permute-done = bf16[1,1,512,2048]{3,2,1,0:T(8,128)(2,1)S(1)} collective-permute-done((bf16[1,1,512,2048]{3,2,1,0:T(8,128)(2,1)}, bf16[1,1,512,2048]{3,2,1,0:T(8,128)(2,1)S(1)}, u32[]{:S(2)}, u32[]{:S(2)}) %collective-permute-start) | collective-permute-done | bytes 2097184 | tf_op jit(solution)/shard_map/ppermute | solution.py:13
  96.5 1.4 copy-done.11
  104.2 6.4 copy.51
  110.6 7.0 all-gather.11.cloned.1.call-done
  117.6 6.4 copy.50
  123.9 76.4 %all-gather.9.cloned.1.call-done = bf16[256,8192]{1,0:T(8,128)(2,1)} async-done(((bf16[256,2048]{1,0:T(8,128)(2,1)}), bf16[256,8192]{1,0:T(8,128)(2,1)}) %all-gather.9.cloned.1.call-update) | async-done | bytes 4194320 | tf_op jit(solution)/shard_map/all_gather | solution.py:84
  200.4 4.9 multiply_reduce_fusion.2
  206.3 1.3 fusion.60
  207.6 2.0 fusion.43
  209.6 140.3 %all-gather.15.cloned.1.call-done = bf16[1,1,512,8192]{3,2,1,0:T(8,128)(2,1)} async-done(((bf16[1,1,512,2048]{3,2,1,0:T(8,128)(2,1)}), bf16[1,1,512,8192]{3,2,1,0:T(8,128)(2,1)}) %all-gather.15.cloned.1.call-update) | async-done | bytes 8388624 | tf_op jit(solution)/shard_map/all_gather | solution.py:57
  350.0 5.1 fusion.1
  355.1 100.4 %all-gather.17.cloned.1.call-done = bf16[1,8192,1024]{2,1,0:T(8,128)(2,1)} async-done(((bf16[1,2048,1024]{2,1,0:T(8,128)(2,1)}), bf16[1,8192,1024]{2,1,0:T(8,128)(2,1)}) %all-gather.17.cloned.1.call-update) | async-done | bytes 16777232 | tf_op jit(solution)/shard_map/all_gather | solution.py:64
  455.5 21.4 %copy.52 = bf16[1024,8192]{1,0:T(8,128)(2,1)} copy(bf16[1024,8192]{0,1:T(8,128)(2,1)} %bitcast.150) | data formatting | bytes 33554432 | tf_op jit(solution)/shard_map/dot_general | solution.py:62
  477.0 14.8 %multiply_reduce_fusion = (f32[512,8]{0,1:T(8,128)S(1)}, f32[512,8,128]{0,2,1:T(8,128)S(1)}) fusion(bf16[8,128,8192]{2,1,0:T(8,128)(2,1)} %bitcast.151, bf16[1,1,512,8192]{3,2,1,0:T(8,128)(2,1)} %all-gather.15.cloned.1.call-done, f32[8192]{0:T(1024)S(1)} %bitcast.169, f32[512]{0:T(512)S(1)} %add_rsqrt_fusion.1), kind=kOutput, calls=%fused_computation.55 | convolution fusion | flops 8607756288 | bytes 27314176 | tf_op jit(solution)/shard_map/dot_general | solution.py:62
  492.3 5.1 fusion.101
  498.1 3.9 fusion.16
  506.2 1.3 fusion.19
  508.4 3.4 fusion.4
  511.9 5.5 convolution_convert_fusion
  517.4 3.2 convolution_convert_fusion.1
  520.6 7.7 %pad_maximum_fusion = bf16[8192,512]{0,1:T(8,128)(2,1)} fusion(bf16[8192,256]{0,1:T(8,128)(2,1)} %convolution_convert_fusion, bf16[8192,256]{0,1:T(8,128)(2,1)} %convolution_convert_fusion.1), kind=kLoop, calls=%fused_computation.13 | loop fusion | flops 16777216 | bytes 16777216 | tf_op jit(solution)/shard_map/concatenate | solution.py:130
  529.1 59.6 %reduce-scatter.4.cloned.1.call-done = bf16[256,2048]{1,0:T(8,128)(2,1)} async-done(((bf16[256,8192]{1,0:T(8,128)(2,1)}), bf16[256,2048]{1,0:T(8,128)(2,1)}) %reduce-scatter.4.cloned.1.call-update) | async-done | bytes 1048592 | tf_op jit(solution)/shard_map/reduce_scatter | solution.py:109
  588.7 6.8 gather_fusion
  595.5 3.7 select_convert_fusion
  600.3 1.2 select_convert_fusion.1
  601.6 62.2 %reduce-scatter.8.cloned.1.call-done = bf16[2048,512]{0,1:T(8,128)(2,1)} async-done(((bf16[8192,512]{0,1:T(8,128)(2,1)}), bf16[2048,512]{0,1:T(8,128)(2,1)}) %reduce-scatter.8.cloned.1.call-update) | async-done | bytes 2097168 | tf_op jit(solution)/shard_map/reduce_scatter | solution.py:129
  663.8 1.7 slice_bitcast_fusion
  665.4 1.3 copy.64
  666.7 1.3 copy.65
  668.0 30.4 %reduce-scatter.6.cloned.1.call-done = bf16[256,2048]{1,0:T(8,128)(2,1)} async-done(((bf16[512,2048]{1,0:T(8,128)(2,1)}), bf16[256,2048]{1,0:T(8,128)(2,1)}) %reduce-scatter.6.cloned.1.call-update) | async-done | bytes 1048592 | tf_op jit(solution)/shard_map/reduce_scatter | solution.py:114
  (81 shorter events, 15.9 us)
Async XLA Ops:
  7.2 2.3 copy-start
  7.2 38.2 %all-gather.7.cloned.1.call-start = ((), (), s32[]{:S(2)}) async-start(), calls=%async_computation.3 | async-start | bytes 3145728 | tf_op jit(solution)/shard_map/all_gather | solution.py:79
  7.9 96.3 %all-gather.13.cloned.1.call-start = ((), (), s32[]{:S(2)}) async-start(), calls=%async_computation.6 | async-start | bytes 5242880 | tf_op jit(solution)/shard_map/all_gather | solution.py:71
  8.7 108.9 %all-gather.11.cloned.1.call-start = ((), (), s32[]{:S(2)}) async-start(), calls=%async_computation.5 | async-start | bytes 5242880 | tf_op jit(solution)/shard_map/all_gather | solution.py:72
  9.4 191.0 %all-gather.9.cloned.1.call-start = ((), (), s32[]{:S(2)}) async-start(), calls=%async_computation.4 | async-start | bytes 5242880 | tf_op jit(solution)/shard_map/all_gather | solution.py:84
  48.8 51.1 %copy-start.12 = (bf16[1,1,512,1024]{3,2,1,0:T(8,128)(2,1)S(1)}, bf16[1,1,512,1024]{3,2,1,0:T(8,128)(2,1)}, u32[]{:S(2)}) copy-start(bf16[1,1,512,1024]{3,2,1,0:T(8,128)(2,1)} %param.25) | copy-start | bytes 3145732
  48.8 301.2 %all-gather.15.cloned.1.call-start = ((), (), s32[]{:S(2)}) async-start(), calls=%async_computation.7 | async-start | bytes 10485760 | tf_op jit(solution)/shard_map/all_gather | solution.py:57
  48.9 47.6 %collective-permute-start = (bf16[1,1,512,2048]{3,2,1,0:T(8,128)(2,1)}, bf16[1,1,512,2048]{3,2,1,0:T(8,128)(2,1)S(1)}, u32[]{:S(2)}, u32[]{:S(2)}) collective-permute-start(bf16[1,1,512,2048]{3,2,1,0:T(8,128)(2,1)} %param.13), channel_id=1, source_target_pairs={{0,16},{16,0},{1,17},{17,1},{2,18},{18,2},{3,19},{19,3},{4,20},{20... | collective-permute-start | bytes 6291464 | tf_op jit(solution)/shard_map/ppermute | solution.py:13
  96.5 1.4 copy-start.11
  97.9 4.5 copy-start.17
  98.0 357.6 %all-gather.17.cloned.1.call-start = ((), (), s32[]{:S(2)}) async-start(), calls=%async_computation.8 | async-start | bytes 20971520 | tf_op jit(solution)/shard_map/all_gather | solution.py:64
  98.5 490.2 %reduce-scatter.4.cloned.1.call-start = ((), (), s32[]{:S(2)}) async-start(), calls=%async_computation.9 | async-start | bytes 5242880 | tf_op jit(solution)/shard_map/reduce_scatter | solution.py:109
  200.4 4.9 copy-start.14
  200.4 5.7 copy-start.5
  200.4 5.9 copy-start.10
  455.5 21.4 %copy-start.16 = (f32[1,8192]{1,0:T(1,128)S(1)}, f32[1,8192]{1,0:T(1,128)}, u32[]{:S(2)}) copy-start(f32[1,8192]{1,0:T(1,128)} %param.18) | copy-start | bytes 98308
  477.0 14.8 %copy-start.15 = (f32[1,128]{1,0:T(1,128)S(1)}, f32[1,128]{1,0:T(1,128)}, u32[]{:S(2)}) copy-start(f32[1,128]{1,0:T(1,128)} %param.22) | copy-start | bytes 1540
  498.1 3.9 copy-start.8
  498.1 4.7 copy-start.9
  498.1 4.7 copy-start.13
  498.1 4.7 copy-start.18
  502.0 2.3 copy-start.2
  504.0 2.2 copy-start.4
  506.2 2.2 copy-start.7
  511.8 151.9 %reduce-scatter.8.cloned.1.call-start = ((), (), s32[]{:S(2)}) async-start(), calls=%async_computation.11 | async-start | bytes 10485760 | tf_op jit(solution)/shard_map/reduce_scatter | solution.py:129
  511.9 5.5 copy-start.6
  528.3 170.1 %reduce-scatter.6.cloned.1.call-start = ((), (), s32[]{:S(2)}) async-start(), calls=%async_computation.10 | async-start | bytes 3145728 | tf_op jit(solution)/shard_map/reduce_scatter | solution.py:114
  595.5 3.7 copy-start.3
  600.3 98.1 %copy-start.1 = (s32[1,2]{1,0:T(1,128)S(1)}, s32[1,2]{1,0:T(1,128)}, u32[]{:S(2)}) copy-start(s32[1,2]{1,0:T(1,128)} %param.17) | copy-start | bytes 28
Sparse Core Ops, SparseCore 0:
  9.6 35.7 all-gather.6
  47.0 34.4 all-gather.12
  83.1 34.4 all-gather.10
  119.6 80.7 all-gather.8
  201.8 148.1 all-gather.14
  351.4 104.1 all-gather.16
  511.9 76.7 reduce-scatter.3
  591.5 72.2 reduce-scatter.7
  666.6 31.8 reduce-scatter.5
where the time goes:
time: 706 us; the launch traced here: 705 us
  waiting for transfers between devices  561 us (79%)
  local copies, waits for them, and re-layouts  51.3 us (7%)
  matrix products  44.1 us (6%)
  other arithmetic  30.3 us (4%)
  between operations  17.4 us (2%)
    all_gather x1, waiting for transfers between devices, per_device(): full_text = lax.all_gather(arrived, 'mp', axis=3, tiled=True)[0, 0]  140 us
    all_gather x1, waiting for transfers between devices, per_device(): lax.all_gather(query_weight, 'dp', axis=1, tiled=True)[0]  100 us
    all_gather x1, waiting for transfers between devices, per_device(): image = lax.all_gather(image_part, 'mp', axis=1, tiled=True)  76.4 us
    reduce_scatter x1, waiting for transfers between devices, per_device(): lax.psum_scatter(jnp.concatenate([key_part, value_part], axis=1).astype(j...  62.2 us
    reduce_scatter x1, waiting for transfers between devices, per_device(): lax.psum_scatter(partial_bf.astype(jnp.float32).astype(jnp.bfloat16), 'mp...  59.6 us
    ppermute x1, waiting for transfers between devices, shifted(): return lax.ppermute(value, axis, pairs)  47.3 us
    all_gather x1, waiting for transfers between devices, per_device(): shard_piece = lax.all_gather(vision, 'section', axis=1, tiled=True)  34.7 us
    reduce_scatter x1, waiting for transfers between devices, per_device(): lax.psum_scatter(jnp.where((row_ids // slot_rows == wanted)[:, None], tak...  30.4 us
  transfers between devices with their start and end apart: 10, of which 9 were waited for; matrix products, arithmetic and copies ran while one was open for 10% of the time, Pallas kernels for 0%

commit v1 on v0

--- a/solution.py
+++ b/solution.py
@@ -54,7 +54,20 @@
     context_grad,
 ):
     arrived = shifted(text_in, "section", 1)
-    full_text = lax.all_gather(arrived, "mp", axis=3, tiled=True)[0, 0]
+
+    def launch_the_case(out_dim, my_data):
+        n = lax.axis_size("mp")
+        column = [(rr, (rr + 1) % n) for rr in range(n)]
+        runs = [(rr, (rr - 1) % n) for rr in range(n)]
+        z2, upper = ([my_data], [my_data])
+        for _ in range(n // 2):
+            z2.append(lax.ppermute(z2[-1], "mp", column))
+        for _ in [*range((n - 1) // 2)]:
+            upper.append(lax.ppermute(upper[-1], "mp", runs))
+        e_now = jnp.concatenate([*z2[::-1], *upper[1:]], out_dim)
+        return jnp.roll(e_now, (lax.axis_index("mp") - n // 2) * my_data.shape[out_dim], out_dim)
+
+    full_text = launch_the_case(3, arrived)[0, 0]
     text_rows = full_text.shape[0]
     normed = norm_rows(full_text, norm_gain[0]).astype(jnp.bfloat16)
     width_q = query_weight.shape[2]

time: 706 us -> 635 us (0.90)
  waiting for transfers between devices: 561 us -> 453 us
  starting transfers between devices: 0.74 us -> 22.1 us
  local copies, waits for them, and re-layouts: 51.3 us -> 69.4 us
    ppermute x0 -> x3, waiting for transfers between devices: none -> 174 us  [the longest x2 138 us: launch_the_case(): z2.append(lax.ppermute(z2[-1], 'mp', column))]
    all_gather x1 -> x0, waiting for transfers between devices: 140 us -> none  [per_device(): full_text = lax.all_gather(arrived, 'mp', axis=3, tiled=True)[0, 0]]
    all_gather x1, waiting for transfers between devices: 76.4 us -> 0.01 us  [per_device(): image = lax.all_gather(image_part, 'mp', axis=1, tiled=True)]
    all_gather x1, waiting for transfers between devices: 100 us -> 42.8 us  [per_device(): lax.all_gather(query_weight, 'dp', axis=1, tiled=True)[0]]
    ppermute x0 -> x3, starting transfers between devices: none -> 21.4 us  [the longest x2 16.2 us: launch_the_case(): z2.append(lax.ppermute(z2[-1], 'mp', column))]
    unnamed x40 -> x49, local copies, waits for them, and re-layouts: 6.98 us -> 23.4 us
  transfers between devices with their start and end apart: 10 -> 12, of which waited for: 9 -> 9; matrix products, arithmetic and copies ran while one was open for 10% -> 12% of each run, Pallas kernels for 0% -> 0%
where the time goes in v1:
time: 635 us; the launch traced here: 634 us
  waiting for transfers between devices  453 us (71%)
  local copies, waits for them, and re-layouts  69.4 us (11%)
  matrix products  44.1 us (7%)
  other arithmetic  26.9 us (4%)
  starting transfers between devices  22.1 us (3%)
  between operations  17.8 us (3%)
    ppermute x2, waiting for transfers between devices, launch_the_case(): z2.append(lax.ppermute(z2[-1], 'mp', column))  138 us
    reduce_scatter x1, waiting for transfers between devices, per_device(): lax.psum_scatter(jnp.concatenate([key_part, value_part], axis=1).astype(j...  62.1 us
    reduce_scatter x1, waiting for transfers between devices, per_device(): lax.psum_scatter(partial_bf.astype(jnp.float32).astype(jnp.bfloat16), 'mp...  59.6 us
    ppermute x1, waiting for transfers between devices, shifted(): return lax.ppermute(value, axis, pairs)  47.2 us
    all_gather x1, waiting for transfers between devices, per_device(): lax.all_gather(query_weight, 'dp', axis=1, tiled=True)[0]  42.8 us
    ppermute x1, waiting for transfers between devices, launch_the_case(): upper.append(lax.ppermute(upper[-1], 'mp', runs))  35.8 us
    all_gather x1, waiting for transfers between devices, per_device(): shard_piece = lax.all_gather(vision, 'section', axis=1, tiled=True)  34.7 us
    reduce_scatter x1, waiting for transfers between devices, per_device(): lax.psum_scatter(jnp.where((row_ids // slot_rows == wanted)[:, None], tak...  30.4 us
  transfers between devices with their start and end apart: 12, of which 9 were waited for; matrix products, arithmetic and copies ran while one was open for 12% of the time, Pallas kernels for 0%

profile of v1, /device:TPU:0, one launch (start us, length us, event | category | flops | bytes accessed | tf_op | source)
XLA Modules:
  0.0 633.5 jit_solution(2979386620248394380)
XLA Ops:
  10.7 34.7 %all-gather.6.cloned.1.call-done = bf16[1,2,256,2048]{3,2,0,1:T(8,128)(2,1)} async-done(((bf16[1,1,256,2048]{3,2,0,1:T(8,128)(2,1)}), bf16[1,2,256,2048]{3,2,0,1:T(8,128)(2,1)}) %all-gather.6.cloned.1.call-update) | async-done | bytes 2097168 | tf_op jit(solution)/shard_map/all_gather | solution.py:92
  45.4 3.4 fusion.35
  49.9 47.2 %collective-permute-done = bf16[1,1,512,2048]{3,2,1,0:T(8,128)(2,1)} collective-permute-done((bf16[1,1,512,2048]{3,2,1,0:T(8,128)(2,1)S(1)}, bf16[1,1,512,2048]{3,2,1,0:T(8,128)(2,1)}, u32[]{:S(2)}, u32[]{:S(2)}) %collective-permute-start) | collective-permute-done | bytes 2097184 | tf_op jit(solution)/shard_map/ppermute | solution.py:13
  98.5 62.3 %collective-permute-done.1 = bf16[1,1,512,2048]{3,2,1,0:T(8,128)(2,1)} collective-permute-done((bf16[1,1,512,2048]{3,2,1,0:T(8,128)(2,1)}, bf16[1,1,512,2048]{3,2,1,0:T(8,128)(2,1)}, u32[]{:S(2)}, u32[]{:S(2)}) %collective-permute-start.1) | collective-permute-done | bytes 2097184 | tf_op jit(solution)/shard_map/ppermute | solution.py:64
  160.8 14.7 %collective-permute-start.2 = (bf16[1,1,512,2048]{3,2,1,0:T(8,128)(2,1)}, bf16[1,1,512,2048]{3,2,1,0:T(8,128)(2,1)}, u32[]{:S(2)}, u32[]{:S(2)}) collective-permute-start(bf16[1,1,512,2048]{3,2,1,0:T(8,128)(2,1)} %collective-permute-done.1), channel_id=1, source_target_pairs={{0,4},{4,8},{8,12},{12,0},{1,5},{5,9},{9,13},{13,1},{2,6},{6,10},{... | collective-permute-start | bytes 6291464 | tf_op jit(solution)/shard_map/ppermute | solution.py:64
  175.6 5.1 collective-permute-start.3
  186.3 75.6 %collective-permute-done.2 = bf16[1,1,512,2048]{3,2,1,0:T(8,128)(2,1)} collective-permute-done((bf16[1,1,512,2048]{3,2,1,0:T(8,128)(2,1)}, bf16[1,1,512,2048]{3,2,1,0:T(8,128)(2,1)}, u32[]{:S(2)}, u32[]{:S(2)}) %collective-permute-start.2) | collective-permute-done | bytes 2097184 | tf_op jit(solution)/shard_map/ppermute | solution.py:64
  263.7 1.7 constant_dynamic-update-slice_fusion.6
  265.4 1.7 constant_dynamic-update-slice_fusion.5
  267.1 35.8 %collective-permute-done.3 = bf16[1,1,512,2048]{3,2,1,0:T(8,128)(2,1)} collective-permute-done((bf16[1,1,512,2048]{3,2,1,0:T(8,128)(2,1)}, bf16[1,1,512,2048]{3,2,1,0:T(8,128)(2,1)}, u32[]{:S(2)}, u32[]{:S(2)}) %collective-permute-start.3) | collective-permute-done | bytes 2097184 | tf_op jit(solution)/shard_map/ppermute | solution.py:66
  304.7 1.7 constant_dynamic-update-slice_fusion.3
  306.4 1.7 constant_dynamic-update-slice_fusion.2
  308.1 1.7 constant_dynamic-update-slice_fusion.1
  311.6 5.7 copy-done.9
  319.1 6.4 %copy.51 = bf16[256,8192]{1,0:T(8,128)(2,1)} copy(bf16[256,8192]{0,1:T(8,128)(2,1)} %bitcast.149) | data formatting | bytes 8388608 | tf_op jit(solution)/shard_map/dot_general | solution.py:99
  325.5 6.4 %copy.50 = bf16[256,8192]{1,0:T(8,128)(2,1)} copy(bf16[256,8192]{0,1:T(8,128)(2,1)} %bitcast.152) | data formatting | bytes 8388608 | tf_op jit(solution)/shard_map/dot_general | solution.py:102
  331.9 4.9 multiply_reduce_fusion.2
  339.1 2.1 fusion.44
  341.2 42.8 %all-gather.14.cloned.1.call-done = bf16[1,8192,1024]{2,1,0:T(8,128)(2,1)} async-done(((bf16[1,2048,1024]{2,1,0:T(8,128)(2,1)}), bf16[1,8192,1024]{2,1,0:T(8,128)(2,1)}) %all-gather.14.cloned.1.call-update) | async-done | bytes 16777232 | tf_op jit(solution)/shard_map/all_gather | solution.py:77
  384.1 21.2 %copy.52 = bf16[1024,8192]{1,0:T(8,128)(2,1)} copy(bf16[1024,8192]{0,1:T(8,128)(2,1)} %bitcast.150) | data formatting | bytes 33554432 | tf_op jit(solution)/shard_map/dot_general | solution.py:75
  405.3 14.8 %multiply_reduce_fusion = (f32[512,8]{0,1:T(8,128)S(1)}, f32[512,8,128]{0,2,1:T(8,128)S(1)}) fusion(bf16[8,128,8192]{2,1,0:T(8,128)(2,1)} %bitcast.151, f32[8192]{0:T(1024)S(1)} %bitcast.169, f32[512]{0:T(512)S(1)} %add_rsqrt_fusion.1, bf16[1,1,512,16384]{3,2,1,0:T(8,128)(2,1)} %copy-done.9, s32[]{:T(128)S(6)} %select_n.103), kind=kOutput, calls=%fused_computation.56 | convolution fusion | flops 8607756288 | bytes 27314180 | tf_op jit(solution)/shard_map/dot_general | solution.py:75
  420.6 5.1 fusion.103
  426.5 3.9 fusion.17
  436.7 3.4 fusion.4
  440.2 5.5 convolution_convert_fusion.1
  445.7 3.2 convolution_convert_fusion
  448.9 7.7 %pad_maximum_fusion = bf16[8192,512]{0,1:T(8,128)(2,1)} fusion(bf16[8192,256]{0,1:T(8,128)(2,1)} %convolution_convert_fusion, bf16[8192,256]{0,1:T(8,128)(2,1)} %convolution_convert_fusion.1), kind=kLoop, calls=%fused_computation.13 | loop fusion | flops 16777216 | bytes 16777216 | tf_op jit(solution)/shard_map/concatenate | solution.py:143
  457.4 59.6 %reduce-scatter.4.cloned.1.call-done = bf16[256,2048]{1,0:T(8,128)(2,1)} async-done(((bf16[256,8192]{1,0:T(8,128)(2,1)}), bf16[256,2048]{1,0:T(8,128)(2,1)}) %reduce-scatter.4.cloned.1.call-update) | async-done | bytes 1048592 | tf_op jit(solution)/shard_map/reduce_scatter | solution.py:122
  517.0 6.8 %gather_fusion = bf16[512,2048]{1,0:T(8,128)(2,1)} fusion(bf16[256,2048]{1,0:T(8,128)(2,1)} %reduce-scatter.4.cloned.1.call-done, s32[1024]{0:T(1024)S(1)} %pad_clamp_fusion), kind=kCustom, calls=%fused_computation | custom fusion | bytes 4196352 | tf_op jit(solution)/shard_map/jit(_take)/gather | solution.py:126
  523.9 3.7 select_convert_fusion
  529.9 62.1 %reduce-scatter.8.cloned.1.call-done = bf16[2048,512]{0,1:T(8,128)(2,1)} async-done(((bf16[8192,512]{0,1:T(8,128)(2,1)}), bf16[2048,512]{0,1:T(8,128)(2,1)}) %reduce-scatter.8.cloned.1.call-update) | async-done | bytes 2097168 | tf_op jit(solution)/shard_map/reduce_scatter | solution.py:142
  596.3 30.4 %reduce-scatter.6.cloned.1.call-done = bf16[256,2048]{1,0:T(8,128)(2,1)} async-done(((bf16[512,2048]{1,0:T(8,128)(2,1)}), bf16[256,2048]{1,0:T(8,128)(2,1)}) %reduce-scatter.6.cloned.1.call-update) | async-done | bytes 1048592 | tf_op jit(solution)/shard_map/reduce_scatter | solution.py:127
  (94 shorter events, 32.4 us)
Async XLA Ops:
  7.2 2.3 copy-start
  7.2 38.2 %all-gather.6.cloned.1.call-start = ((), (), s32[]{:S(2)}) async-start(), calls=%async_computation.3 | async-start | bytes 3145728 | tf_op jit(solution)/shard_map/all_gather | solution.py:92
  7.9 311.2 %all-gather.12.cloned.1.call-start = ((), (), s32[]{:S(2)}) async-start(), calls=%async_computation.6 | async-start | bytes 5242880 | tf_op jit(solution)/shard_map/all_gather | solution.py:84
  8.7 316.9 %all-gather.10.cloned.1.call-start = ((), (), s32[]{:S(2)}) async-start(), calls=%async_computation.5 | async-start | bytes 5242880 | tf_op jit(solution)/shard_map/all_gather | solution.py:85
  9.4 322.5 %all-gather.8.cloned.1.call-start = ((), (), s32[]{:S(2)}) async-start(), calls=%async_computation.4 | async-start | bytes 5242880 | tf_op jit(solution)/shard_map/all_gather | solution.py:97
  10.7 38.8 %copy-start.16 = (bf16[1,1,512,2048]{3,2,1,0:T(8,128)(2,1)S(1)}, bf16[1,1,512,2048]{3,2,1,0:T(8,128)(2,1)}, u32[]{:S(2)}) copy-start(bf16[1,1,512,2048]{3,2,1,0:T(8,128)(2,1)} %param.13) | copy-start | bytes 6291460
  10.7 172.6 %copy-start.12 = (bf16[1,1,512,1024]{3,2,1,0:T(8,128)(2,1)S(1)}, bf16[1,1,512,1024]{3,2,1,0:T(8,128)(2,1)}, u32[]{:S(2)}) copy-start(bf16[1,1,512,1024]{3,2,1,0:T(8,128)(2,1)} %param.25) | copy-start | bytes 3145732
  48.8 135.7 %copy-start.18 = (s32[1,2]{1,0:T(1,128)S(1)}, s32[1,2]{1,0:T(1,128)}, u32[]{:S(2)}) copy-start(s32[1,2]{1,0:T(1,128)} %param.15) | copy-start | bytes 28
  48.8 335.2 %all-gather.14.cloned.1.call-start = ((), (), s32[]{:S(2)}) async-start(), calls=%async_computation.7 | async-start | bytes 20971520 | tf_op jit(solution)/shard_map/all_gather | solution.py:77
  49.4 467.6 %reduce-scatter.4.cloned.1.call-start = ((), (), s32[]{:S(2)}) async-start(), calls=%async_computation.8 | async-start | bytes 5242880 | tf_op jit(solution)/shard_map/reduce_scatter | solution.py:122
  49.5 47.5 %collective-permute-start = (bf16[1,1,512,2048]{3,2,1,0:T(8,128)(2,1)S(1)}, bf16[1,1,512,2048]{3,2,1,0:T(8,128)(2,1)}, u32[]{:S(2)}, u32[]{:S(2)}) collective-permute-start(bf16[1,1,512,2048]{3,2,1,0:T(8,128)(2,1)S(1)} %copy-done.16), channel_id=1, source_target_pairs={{0,16},{16,0},{1,17},{17,1},{2,18},{18,2},{3,19},{19,3},{4,20},{20... | collective-permute-start | bytes 6291464 | tf_op jit(solution)/shard_map/ppermute | solution.py:13
  97.0 63.8 %collective-permute-start.1 = (bf16[1,1,512,2048]{3,2,1,0:T(8,128)(2,1)}, bf16[1,1,512,2048]{3,2,1,0:T(8,128)(2,1)}, u32[]{:S(2)}, u32[]{:S(2)}) collective-permute-start(bf16[1,1,512,2048]{3,2,1,0:T(8,128)(2,1)} %collective-permute-done), channel_id=1, source_target_pairs={{0,4},{4,8},{8,12},{12,0},{1,5},{5,9},{9,13},{13,1},{2,6},{6,10},{... | collective-permute-start | bytes 6291464 | tf_op jit(solution)/shard_map/ppermute | solution.py:64
  160.8 101.1 %collective-permute-start.2 = (bf16[1,1,512,2048]{3,2,1,0:T(8,128)(2,1)}, bf16[1,1,512,2048]{3,2,1,0:T(8,128)(2,1)}, u32[]{:S(2)}, u32[]{:S(2)}) collective-permute-start(bf16[1,1,512,2048]{3,2,1,0:T(8,128)(2,1)} %collective-permute-done.1), channel_id=1, source_target_pairs={{0,4},{4,8},{8,12},{12,0},{1,5},{5,9},{9,13},{13,1},{2,6},{6,10},{... | collective-permute-start | bytes 6291464 | tf_op jit(solution)/shard_map/ppermute | solution.py:64
  175.6 127.4 %collective-permute-start.3 = (bf16[1,1,512,2048]{3,2,1,0:T(8,128)(2,1)}, bf16[1,1,512,2048]{3,2,1,0:T(8,128)(2,1)}, u32[]{:S(2)}, u32[]{:S(2)}) collective-permute-start(bf16[1,1,512,2048]{3,2,1,0:T(8,128)(2,1)} %collective-permute-done), channel_id=1, source_target_pairs={{0,12},{4,0},{8,4},{12,8},{1,13},{5,1},{9,5},{13,9},{2,14},{6,2},{... | collective-permute-start | bytes 6291464 | tf_op jit(solution)/shard_map/ppermute | solution.py:66
  311.6 5.7 copy-start.9
  331.9 4.9 copy-start.14
  331.9 5.7 copy-start.5
  331.9 5.9 copy-start.11
  384.1 21.2 %copy-start.17 = (f32[1,8192]{1,0:T(1,128)S(1)}, f32[1,8192]{1,0:T(1,128)}, u32[]{:S(2)}) copy-start(f32[1,8192]{1,0:T(1,128)} %param.18) | copy-start | bytes 98308
  405.3 14.8 %copy-start.15 = (f32[1,128]{1,0:T(1,128)S(1)}, f32[1,128]{1,0:T(1,128)}, u32[]{:S(2)}) copy-start(f32[1,128]{1,0:T(1,128)} %param.22) | copy-start | bytes 1540
  426.4 3.9 copy-start.8
  426.4 4.7 copy-start.10
  426.4 4.7 copy-start.13
  426.4 4.7 copy-start.19
  430.3 2.3 copy-start.2
  432.3 2.2 copy-start.4
  434.5 2.2 copy-start.7
  440.1 151.9 %reduce-scatter.8.cloned.1.call-start = ((), (), s32[]{:S(2)}) async-start(), calls=%async_computation.10 | async-start | bytes 10485760 | tf_op jit(solution)/shard_map/reduce_scatter | solution.py:142
  440.2 5.6 copy-start.6
  456.6 170.1 %reduce-scatter.6.cloned.1.call-start = ((), (), s32[]{:S(2)}) async-start(), calls=%async_computation.9 | async-start | bytes 3145728 | tf_op jit(solution)/shard_map/reduce_scatter | solution.py:127
  523.9 3.7 copy-start.3
  528.7 98.0 %copy-start.1 = (s32[1,2]{1,0:T(1,128)S(1)}, s32[1,2]{1,0:T(1,128)}, u32[]{:S(2)}) copy-start(s32[1,2]{1,0:T(1,128)} %param.17) | copy-start | bytes 28
Sparse Core Ops, SparseCore 0:
  9.6 35.7 all-gather.5
  47.0 34.4 all-gather.11
  83.1 34.4 all-gather.9
  119.6 159.2 all-gather.7
  280.2 103.7 all-gather.13
  440.2 76.7 reduce-scatter.3
  519.8 72.2 reduce-scatter.7
  594.8 31.8 reduce-scatter.5
